TPU v7x, 32 devices: a whole 2x2x4 slice. The times are simulated.
32 devices in a mesh: group: 4 (over z), member: 8 (over y, x, core).
Axes of the slice: x: 2, y: 2, z: 4, core: 2. Of those that a mesh axis runs over, the one named last changes fastest.
Arguments:
- query_feat: bfloat16 [4096, 4096], P(('group', 'member'))
- code_feat: bfloat16 [4096, 4096], P(('group', 'member'))
- projection: bfloat16 [4096, 1024], replicated
- hard_ids: int32 [32, 16], P(('group', 'member')), may hold values from 0 to 63, as said below
- loss_weight: float32 [4096], P(('group', 'member')), may hold values from 1 to 4
Outputs:
- query_grad: bfloat16 [4096, 4096], P(('group', 'member'))
- code_grad: bfloat16 [4096, 4096], P(('group', 'member'))
- projection_grad: float32 [4096, 1024], P(('group', 'member'))
Inputs may be any that keep to these rules, and one draw needn't show every extreme that they name: `hard_ids`: entry (owner device g * 8 + m) * 2 + slot names code rows of that device. A row names 16 different blocks, none of its own group; at most 8 of them lie in one group, and exactly 8 in some group of every row.
All inputs are finite; a program needn't handle non-finite values.
Results may differ from a plain program's by a relative error of at most 0.02.
Values may be sent and summed in bfloat16 or wider, within the bound.
No kernel may reach another device: no remote copies, remote signals or barrier semaphores. Data moves between devices by JAX's collectives and lax.ppermute only.
A program may use at most 128 MiB of HBM per device.

v0:
```python
import jax
import jax.numpy as jnp
from jax import lax
from jax.sharding import PartitionSpec as P

CB = 64
inverse_temp = 120.0
epsilon = 1e-06


def embed(features, projection):
    values = jnp.dot(features, projection, preferred_element_type=jnp.float32)
    inverse = lax.rsqrt(jnp.sum(values * values, axis=1) + epsilon)
    unit_vec = values * inverse[:, None]
    return (unit_vec, inverse, unit_vec.astype(jnp.bfloat16))


def norm_back(upstream, unit_vec, inverse):
    inner_prod = jnp.sum(unit_vec * upstream, axis=1, keepdims=True)
    return (inverse[:, None] * (upstream - unit_vec * inner_prod)).astype(jnp.bfloat16)


def shift_all(x, axis):
    size = lax.axis_size(axis)
    index = lax.axis_index(axis)
    got = [x]
    for s in range(1, size):
        got.append(lax.ppermute(x, axis, [(i, (i + s) % size) for i in range(size)]))
    order = (index - jnp.arange(size)) % size
    return jax.tree.map(lambda *xs: jnp.take(jnp.stack(xs, axis=0), order, axis=0), *got)


def exchange(parts, axis):
    size = lax.axis_size(axis)
    index = lax.axis_index(axis)
    got = [jnp.take(parts, index, axis=0)]
    for s in range(1, size):
        sent = jnp.take(parts, (index + s) % size, axis=0)
        got.append(lax.ppermute(sent, axis, [(i, (i + s) % size) for i in range(size)]))
    stacked = jnp.stack(got, axis=0)
    return jnp.take(stacked, (index - jnp.arange(size)) % size, axis=0)


def body(query_feat, code_feat, projection, hard_ids, loss_weight):
    groups = lax.axis_size("group")
    members = lax.axis_size("member")
    group_index = lax.axis_index("group")
    member_index = lax.axis_index("member")
    queries_dev = query_feat.shape[0]
    feat_width = query_feat.shape[1]
    emb_width = projection.shape[1]
    slot_count = queries_dev // CB
    per_group = members * slot_count
    group_span = members * queries_dev
    rows_dev = feat_width // (groups * members)
    feats = jnp.stack([query_feat, code_feat], axis=0).reshape(
        2, queries_dev, groups, members, rows_dev
    )
    feats = jnp.transpose(feats, (3, 0, 1, 2, 4))
    feat_cols = lax.all_to_all(feats, "member", split_axis=0, concat_axis=0, tiled=True)
    q_unit, q_inv, q_emb = embed(query_feat, projection)
    code_values = lax.all_gather(
        jnp.dot(code_feat, projection, preferred_element_type=jnp.float32),
        "member",
        axis=0,
        tiled=True,
    )
    c_inv = lax.rsqrt(jnp.sum(code_values * code_values, axis=1) + epsilon)
    c_unit = code_values * c_inv[:, None]
    group_codes = c_unit.astype(jnp.bfloat16)
    q_all = lax.all_to_all(
        jnp.broadcast_to(q_emb[None], (groups, queries_dev, emb_width)),
        "group",
        split_axis=0,
        concat_axis=0,
        tiled=True,
    )
    ids_all = shift_all(hard_ids[0], "group")
    block_ids = group_index * per_group + jnp.arange(per_group, dtype=jnp.int32)
    asked = jnp.any(ids_all[:, :, None] == block_ids[None, None, :], axis=1)
    own = jnp.arange(groups, dtype=jnp.int32) == group_index
    block_mask = asked | own[:, None]
    col_mask = jnp.broadcast_to(block_mask[:, :, None], (groups, per_group, CB)).reshape(
        groups, 1, group_span
    )
    scores = inverse_temp * jnp.einsum(
        "gqe,ke->gqk", q_all, group_codes, preferred_element_type=jnp.float32
    )
    scores = jnp.where(col_mask, scores, -jnp.inf)
    part_max = jnp.max(scores, axis=2)
    safe_max = jnp.where(part_max > -jnp.inf, part_max, 0.0)
    part_sum = jnp.sum(jnp.exp(scores - safe_max[:, :, None]), axis=2)
    weights_row = jnp.broadcast_to(loss_weight[None], (groups, queries_dev))
    stats = shift_all(jnp.stack([part_max, part_sum, weights_row], axis=0), "group")
    w_all = stats[:, 2, 0]
    row_max = jnp.max(stats[:, 0], axis=0)
    row_sum = jnp.sum(stats[:, 1] * jnp.exp(stats[:, 0] - row_max[None]), axis=0)
    log_total = row_max + jnp.log(row_sum)
    offsets = jnp.arange(queries_dev, dtype=jnp.int32)
    columns = jnp.arange(group_span, dtype=jnp.int32)
    positive = (columns[None, :] == (member_index * queries_dev + offsets)[:, None]).astype(
        jnp.float32
    )
    positive = positive[None] * own[:, None, None].astype(jnp.float32)
    factor = w_all * inverse_temp
    grad = (factor[:, :, None] * (jnp.exp(scores - log_total[:, :, None]) - positive)).astype(
        jnp.bfloat16
    )
    code_terms = None
    for g in range(groups):
        term = jnp.dot(grad[g].T, q_all[g], preferred_element_type=jnp.float32)
        term = jnp.where(g == group_index, term, term.astype(jnp.bfloat16).astype(jnp.float32))
        code_terms = term if code_terms is None else code_terms + term
    code_sum = code_terms.astype(jnp.bfloat16)
    grad_dq, code_sum = lax.optimization_barrier((grad, code_sum))
    code_delta = lax.psum(code_sum, "member").astype(jnp.float32)
    delta_parts = jnp.einsum(
        "gqk,ke->gqe", grad_dq, group_codes, preferred_element_type=jnp.float32
    )
    returned = exchange(delta_parts.astype(jnp.bfloat16), "group").astype(jnp.float32)
    own_part = jnp.take(delta_parts, group_index, axis=0)
    query_delta = own_part + jnp.sum(jnp.where(own[:, None, None], 0.0, returned), axis=0)
    dz_query = norm_back(query_delta, q_unit, q_inv)
    dz_code_all = norm_back(code_delta, c_unit, c_inv)
    dz_code = lax.dynamic_slice_in_dim(dz_code_all, member_index * queries_dev, queries_dev, 0)
    query_grad = jnp.einsum(
        "qe,de->qd", dz_query, projection, preferred_element_type=jnp.float32
    ).astype(jnp.bfloat16)
    code_grad = jnp.einsum(
        "qe,de->qd", dz_code, projection, preferred_element_type=jnp.float32
    ).astype(jnp.bfloat16)
    dzq_all = lax.all_to_all(
        jnp.broadcast_to(dz_query[None], (members, queries_dev, emb_width)),
        "member",
        split_axis=0,
        concat_axis=0,
        tiled=True,
    )
    dzc_all = dz_code_all.reshape(members, queries_dev, emb_width)
    proj_parts = jnp.einsum(
        "mqgr,mqe->gre", feat_cols[:, 0], dzq_all, preferred_element_type=jnp.float32
    ) + jnp.einsum("mqgr,mqe->gre", feat_cols[:, 1], dzc_all, preferred_element_type=jnp.float32)
    own_proj = jnp.take(proj_parts, group_index, axis=0)
    sent_proj = jnp.where(own[:, None, None], 0.0, proj_parts).astype(jnp.bfloat16)
    projection_grad = own_proj + lax.psum_scatter(
        sent_proj, "group", scatter_dimension=0, tiled=True
    ).reshape(rows_dev, emb_width).astype(jnp.float32)
    return (query_grad, code_grad, projection_grad)


def solution(mesh):
    return jax.shard_map(
        body,
        mesh=mesh,
        in_specs=(
            P(("group", "member"), None),
            P(("group", "member"), None),
            P(),
            P(("group", "member"), None),
            P(("group", "member")),
        ),
        out_specs=(
            P(("group", "member"), None),
            P(("group", "member"), None),
            P(("group", "member"), None),
        ),
        check_vma=False,
    )
```

profile of v0, /device:TPU:0, one launch (start us, length us, event | category | flops | bytes accessed | tf_op | source)
XLA Modules:
  0.0 204.6 jit_solution(2245639925189366476)
XLA Ops:
  7.2 5.8 %fusion.26 = f32[128,1024]{1,0:T(8,128)} fusion(bf16[128,4096]{1,0:T(8,128)(2,1)} %param.10, bf16[4096,1024]{1,0:T(8,128)(2,1)} %param.11), kind=kOutput, calls=%fused_computation.91 | convolution fusion | flops 1073741824 | bytes 9961472 | tf_op jit(solution)/shard_map/dot_general | solution.py:63
  13.1 3.1 %collective-permute-start = (s32[16]{0:T(128)S(1)}, s32[16]{0:T(128)S(1)}, u32[]{:S(2)}, u32[]{:S(2)}) collective-permute-start(s32[16]{0:T(128)S(1)} %bitcast.128), channel_id=1, source_target_pairs={{0,8},{8,16},{16,24},{24,0},{1,9},{9,17},{17,25},{25,1},{2,10},{10... | collective-permute-start | bytes 200 | tf_op jit(solution)/shard_map/ppermute | solution.py:28
  16.2 2.6 %collective-permute-start.1 = (s32[16]{0:T(128)S(1)}, s32[16]{0:T(128)S(1)}, u32[]{:S(2)}, u32[]{:S(2)}) collective-permute-start(s32[16]{0:T(128)S(1)} %bitcast.129), channel_id=1, source_target_pairs={{0,16},{8,24},{16,0},{24,8},{1,17},{9,25},{17,1},{25,9},{2,18},{10... | collective-permute-start | bytes 200 | tf_op jit(solution)/shard_map/ppermute | solution.py:28
  20.2 5.0 %multiply_reduce_fusion.2 = (f32[128]{0:T(128)S(1)}, f32[128,1024]{1,0:T(8,128)S(1)}) fusion(bf16[128,4096]{1,0:T(8,128)(2,1)S(1)} %copy-done.5, bf16[4096,1024]{1,0:T(8,128)(2,1)} %param.11), kind=kOutput, calls=%fused_computation.31 | convolution fusion | flops 1074003840 | bytes 9961984 | tf_op jit(solution)/shard_map/dot_general | solution.py:12
  26.4 3.6 %all-to-all-start = ((bf16[4,128,1024]{2,1,0:T(8,128)(2,1)}), bf16[4,128,1024]{2,1,0:T(8,128)(2,1)S(1)}, u32[]{:S(2)}, u32[]{:S(2)}) async-start(bf16[4,128,1024]{2,1,0:T(8,128)(2,1)} %broadcast_in_dim.126), calls=%async_computation | async-start | bytes 2097152 | tf_op jit(solution)/shard_map/all_to_all | solution.py:71
  37.5 15.0 %all-gather.2.cloned.1.call-done = f32[1024,1024]{1,0:T(8,128)} async-done(((f32[128,1024]{1,0:T(8,128)}), f32[1024,1024]{1,0:T(8,128)}) %all-gather.2.cloned.1.call-update) | async-done | bytes 4194320 | tf_op jit(solution)/shard_map/all_gather | solution.py:62
  52.6 2.5 %multiply_reduce_fusion = f32[1024]{0:T(1024)S(1)} fusion(f32[1024,1024]{1,0:T(8,128)} %all-gather.2.cloned.1.call-done), kind=kLoop, calls=%fused_computation.11 | loop fusion | flops 2096128 | bytes 4198400 | tf_op jit(solution)/shard_map/reduce_sum | solution.py:68
  55.1 4.4 %all-to-all-start.1 = ((bf16[8,2,128,4,128]{2,4,3,1,0:T(8,128)(2,1)}), bf16[8,2,128,4,128]{2,4,3,1,0:T(8,128)(2,1)}, u32[]{:S(2)}, u32[]{:S(2)}) async-start(bf16[8,2,128,4,128]{2,4,3,1,0:T(8,128)(2,1)} %copy.25), calls=%async_computation.1 | async-start | bytes 4194304 | tf_op jit(solution)/shard_map/all_to_all | solution.py:60
  59.5 3.6 %fusion.24 = (f32[4,128]{1,0:T(4,128)S(1)}, f32[4,128,1024]{2,1,0:T(8,128)S(1)}) fusion(bf16[4,128,1024]{2,1,0:T(8,128)(2,1)S(1)} %all-to-all-done, f32[1024,1024]{1,0:T(8,128)} %all-gather.2.cloned.1.call-done, f32[1024]{0:T(1024)S(1)} %add_rsqrt_fusion, pred[4,1024]{1,0:T(4,128)(4,1)S(1)} %broadcast_in_dim.124), kind=kOutput, calls=%fused_computation.89 | convolution fusion | flops 1077411328 | bytes 7350272 | tf_op jit(solution)/shard_map/gqe,ke->gqk/dot_general | solution.py:86
  69.9 3.2 %collective-permute-done.3 = f32[3,4,128]{2,1,0:T(4,128)S(1)} collective-permute-done((f32[3,4,128]{2,1,0:T(4,128)S(1)}, f32[3,4,128]{2,1,0:T(4,128)S(1)}, u32[]{:S(2)}, u32[]{:S(2)}) %collective-permute-start.3) | collective-permute-done | bytes 6176 | tf_op jit(solution)/shard_map/ppermute | solution.py:28
  80.1 3.8 %fusion.25 = (bf16[4,128,1024]{2,1,0:T(8,128)(2,1)S(1)}, f32[4,128,1024]{2,1,0:T(8,128)S(1)}) fusion(bf16[4,128,1024]{2,1,0:T(8,128)(2,1)} %copy-done.1, f32[1024,1024]{1,0:T(8,128)} %all-gather.2.cloned.1.call-done, f32[1024]{0:T(1024)S(1)} %add_rsqrt_fusion), kind=kOutput, calls=%fused_computation.90 | convolution fusion | flops 1076363264 | bytes 8392704 | tf_op jit(solution)/shard_map/gqk,ke->gqe/dot_general | solution.py:117
  85.4 3.3 %collective-permute-start.8 = (bf16[128,1024]{1,0:T(8,128)(2,1)}, bf16[128,1024]{1,0:T(8,128)(2,1)S(1)}, u32[]{:S(2)}, u32[]{:S(2)}) collective-permute-start(bf16[128,1024]{1,0:T(8,128)(2,1)} %get-tuple-element.34), channel_id=1, source_target_pairs={{0,24},{8,0},{16,8},{24,16},{1,25},{9,1},{17,9},{25,17},{2,26},{10... | collective-permute-start | bytes 786440 | tf_op jit(solution)/shard_map/ppermute | solution.py:39
  88.7 7.4 %collective-permute-done.6 = bf16[128,1024]{1,0:T(8,128)(2,1)S(1)} collective-permute-done((bf16[128,1024]{1,0:T(8,128)(2,1)}, bf16[128,1024]{1,0:T(8,128)(2,1)S(1)}, u32[]{:S(2)}, u32[]{:S(2)}) %collective-permute-start.6) | collective-permute-done | bytes 262176 | tf_op jit(solution)/shard_map/ppermute | solution.py:39
  96.2 8.9 %collective-permute-done.7 = bf16[128,1024]{1,0:T(8,128)(2,1)S(1)} collective-permute-done((bf16[128,1024]{1,0:T(8,128)(2,1)}, bf16[128,1024]{1,0:T(8,128)(2,1)S(1)}, u32[]{:S(2)}, u32[]{:S(2)}) %collective-permute-start.7) | collective-permute-done | bytes 262176 | tf_op jit(solution)/shard_map/ppermute | solution.py:39
  106.2 2.9 %gather_fusion.2 = bf16[4,128,1024]{2,1,0:T(8,128)(2,1)} fusion(bf16[4,128,1024]{2,1,0:T(8,128)(2,1)} %pad_maximum_fusion, s32[1024]{0:T(1024)S(1)} %pad_clamp_fusion), kind=kCustom, calls=%fused_computation.2 | custom fusion | bytes 2097168 | tf_op jit(solution)/shard_map/jit(_take)/gather | solution.py:41
  112.7 4.3 %all-to-all-start.2 = ((bf16[8,128,1024]{2,1,0:T(8,128)(2,1)}), bf16[8,128,1024]{2,1,0:T(8,128)(2,1)}, u32[]{:S(2)}, u32[]{:S(2)}) async-start(bf16[8,128,1024]{2,1,0:T(8,128)(2,1)} %broadcast_in_dim.134), calls=%async_computation.2 | async-start | bytes 4194304 | tf_op jit(solution)/shard_map/all_to_all | solution.py:132
  117.1 2.8 %fusion.23 = (bf16[8,1,128,4,128]{2,4,3,1,0:T(8,128)(2,1)S(1)}, bf16[8,1,128,4,128]{2,4,3,1,0:T(8,128)(2,1)}) fusion(bf16[8,2,128,4,128]{2,4,3,1,0:T(8,128)(2,1)} %all-to-all-done.1), kind=kLoop, calls=%fused_computation.88 | loop fusion | bytes 4194304 | tf_op jit(solution)/shard_map/slice | solution.py:142
  119.9 37.8 %all-reduce.2.cloned.1.call-done = bf16[1024,1024]{1,0:T(8,128)(2,1)} async-done(((bf16[1024,1024]{1,0:T(8,128)(2,1)}), bf16[1024,1024]{1,0:T(8,128)(2,1)}) %all-reduce.2.cloned.1.call-update) | async-done | bytes 2097168 | tf_op jit(solution)/shard_map/psum | solution.py:116
  157.7 3.7 %fusion = f32[1024]{0:T(1024)S(1)} fusion(bf16[1024,1024]{1,0:T(8,128)(2,1)} %all-reduce.2.cloned.1.call-done, f32[1024,1024]{1,0:T(8,128)} %all-gather.2.cloned.1.call-done, f32[1024]{0:T(1024)S(1)} %add_rsqrt_fusion), kind=kLoop, calls=%fused_computation.7 | loop fusion | flops 4193280 | bytes 6299648 | tf_op jit(solution)/shard_map/reduce_sum | solution.py:19
  163.2 3.2 %fusion.4 = f32[4,128,1024,1]{2,1,3,0:T(8,128)S(1)} fusion(bf16[8,128,1024]{2,1,0:T(8,128)(2,1)} %all-to-all-done.2, bf16[8,1,128,4,128]{2,4,3,1,0:T(8,128)(2,1)} %get-tuple-element.32), kind=kOutput, calls=%fused_computation.16 | convolution fusion | flops 1073741824 | bytes 5242880 | tf_op jit(solution)/shard_map/mqgr,mqe->gre/dot_general | solution.py:140
  166.4 2.9 %select_convert_fusion = (bf16[4,128,1024]{2,1,0:T(8,128)(2,1)}, f32[4,128,1024]{2,1,0:T(8,128)}) fusion(pred[4]{0:T(512)(128)(4,1)S(1)} %iota_compare_fusion.1, bf16[8,128,1024,1]{2,1,0,3:T(8,128)(2,1)S(1)} %bitcast.116, bf16[8,1,128,4,128]{2,4,3,1,0:T(8,128)(2,1)S(1)} %get-tuple-element.31, f32[4,128,1024,1]{2,1,3,0:T(8,128)S(1)} %fusion.4), kind=kOutput, calls=%fused_computation.18 | convolution fusion | flops 1074790400 | bytes 8388612 | tf_op jit(solution)/shard_map/mqgr,mqe->gre/dot_general | solution.py:142
  169.3 7.2 %convolution_convert_fusion.1 = bf16[128,4096]{1,0:T(8,128)(2,1)} fusion(bf16[128,1024]{1,0:T(8,128)(2,1)S(1)} %multiply_convert_fusion.2, bf16[4096,1024]{1,0:T(8,128)(2,1)} %param.11), kind=kOutput, calls=%fused_computation.6 | convolution fusion | flops 1074266112 | bytes 9699328 | tf_op jit(solution)/shard_map/qe,de->qd/dot_general | solution.py:126
  176.6 7.2 %convolution_convert_fusion = bf16[128,4096]{1,0:T(8,128)(2,1)} fusion(bf16[4096,1024]{1,0:T(8,128)(2,1)} %param.11, bf16[1024,1024]{1,0:T(8,128)(2,1)S(1)} %fusion.2, s32[]{:T(128)S(6)} %select_n.153), kind=kOutput, calls=%fused_computation.5 | convolution fusion | flops 1074266112 | bytes 9699332 | tf_op jit(solution)/shard_map/qe,de->qd/dot_general | solution.py:129
  183.8 12.3 %reduce-scatter.2.cloned.1.call-done = bf16[1,128,1024]{2,1,0:T(8,128)(2,1)} async-done(((bf16[4,128,1024]{2,1,0:T(8,128)(2,1)}), bf16[1,128,1024]{2,1,0:T(8,128)(2,1)}) %reduce-scatter.2.cloned.1.call-update) | async-done | bytes 262160 | tf_op jit(solution)/shard_map/reduce_scatter | solution.py:145
  (88 shorter events, 33.8 us)
Async XLA Ops:
  7.2 5.9 %copy-start.9 = (s32[1,16]{1,0:T(1,128)S(1)}, s32[1,16]{1,0:T(1,128)}, u32[]{:S(2)}) copy-start(s32[1,16]{1,0:T(1,128)} %param.12) | copy-start | bytes 196
  7.2 13.0 %copy-start.5 = (bf16[128,4096]{1,0:T(8,128)(2,1)S(1)}, bf16[128,4096]{1,0:T(8,128)(2,1)}, u32[]{:S(2)}) copy-start(bf16[128,4096]{1,0:T(8,128)(2,1)} %param.9) | copy-start | bytes 3145732
  7.2 45.4 %all-gather.2.cloned.1.call-start = ((), (), s32[]{:S(2)}) async-start(), calls=%async_computation.4 | async-start | bytes 4718592 | tf_op jit(solution)/shard_map/all_gather | solution.py:62
  13.1 23.4 %collective-permute-start = (s32[16]{0:T(128)S(1)}, s32[16]{0:T(128)S(1)}, u32[]{:S(2)}, u32[]{:S(2)}) collective-permute-start(s32[16]{0:T(128)S(1)} %bitcast.128), channel_id=1, source_target_pairs={{0,8},{8,16},{16,24},{24,0},{1,9},{9,17},{17,25},{25,1},{2,10},{10... | collective-permute-start | bytes 200 | tf_op jit(solution)/shard_map/ppermute | solution.py:28
  16.2 20.3 %collective-permute-start.1 = (s32[16]{0:T(128)S(1)}, s32[16]{0:T(128)S(1)}, u32[]{:S(2)}, u32[]{:S(2)}) collective-permute-start(s32[16]{0:T(128)S(1)} %bitcast.129), channel_id=1, source_target_pairs={{0,16},{8,24},{16,0},{24,8},{1,17},{9,25},{17,1},{25,9},{2,18},{10... | collective-permute-start | bytes 200 | tf_op jit(solution)/shard_map/ppermute | solution.py:28
  18.8 17.7 %collective-permute-start.2 = (s32[16]{0:T(128)S(1)}, s32[16]{0:T(128)S(1)}, u32[]{:S(2)}, u32[]{:S(2)}) collective-permute-start(s32[16]{0:T(128)S(1)} %bitcast.130), channel_id=1, source_target_pairs={{0,24},{8,0},{16,8},{24,16},{1,25},{9,1},{17,9},{25,17},{2,26},{10... | collective-permute-start | bytes 200 | tf_op jit(solution)/shard_map/ppermute | solution.py:28
  25.1 1.2 copy-start.3
  26.4 5.1 %copy-start.6 = (bf16[128,4096]{1,0:T(8,128)(2,1)S(1)}, bf16[128,4096]{1,0:T(8,128)(2,1)}, u32[]{:S(2)}) copy-start(bf16[128,4096]{1,0:T(8,128)(2,1)} %param.10) | copy-start | bytes 3145732
  26.4 28.7 %all-to-all-start = ((bf16[4,128,1024]{2,1,0:T(8,128)(2,1)}), bf16[4,128,1024]{2,1,0:T(8,128)(2,1)S(1)}, u32[]{:S(2)}, u32[]{:S(2)}) async-start(bf16[4,128,1024]{2,1,0:T(8,128)(2,1)} %broadcast_in_dim.126), calls=%async_computation | async-start | bytes 2097152 | tf_op jit(solution)/shard_map/all_to_all | solution.py:71
  31.4 1.3 copy-start.7
  55.1 56.0 %all-to-all-start.1 = ((bf16[8,2,128,4,128]{2,4,3,1,0:T(8,128)(2,1)}), bf16[8,2,128,4,128]{2,4,3,1,0:T(8,128)(2,1)}, u32[]{:S(2)}, u32[]{:S(2)}) async-start(bf16[8,2,128,4,128]{2,4,3,1,0:T(8,128)(2,1)} %copy.25), calls=%async_computation.1 | async-start | bytes 4194304 | tf_op jit(solution)/shard_map/all_to_all | solution.py:60
  59.5 98.2 %all-reduce.2.cloned.1.call-start = ((), (), s32[]{:S(2)}) async-start(), calls=%async_computation.5 | async-start | bytes 4194304 | tf_op jit(solution)/shard_map/psum | solution.py:116
  63.8 4.6 %collective-permute-start.4 = (f32[3,4,128]{2,1,0:T(4,128)S(1)}, f32[3,4,128]{2,1,0:T(4,128)S(1)}, u32[]{:S(2)}, u32[]{:S(2)}) collective-permute-start(f32[3,4,128]{2,1,0:T(4,128)S(1)} %get-tuple-element.38), channel_id=1, source_target_pairs={{0,16},{8,24},{16,0},{24,8},{1,17},{9,25},{17,1},{25,9},{2,18},{10... | collective-permute-start | bytes 18440 | tf_op jit(solution)/shard_map/ppermute | solution.py:28
  66.3 3.6 %collective-permute-start.5 = (f32[3,4,128]{2,1,0:T(4,128)S(1)}, f32[3,4,128]{2,1,0:T(4,128)S(1)}, u32[]{:S(2)}, u32[]{:S(2)}) collective-permute-start(f32[3,4,128]{2,1,0:T(4,128)S(1)} %get-tuple-element.38), channel_id=1, source_target_pairs={{0,24},{8,0},{16,8},{24,16},{1,25},{9,1},{17,9},{25,17},{2,26},{10... | collective-permute-start | bytes 18440 | tf_op jit(solution)/shard_map/ppermute | solution.py:28
  67.7 5.4 %collective-permute-start.3 = (f32[3,4,128]{2,1,0:T(4,128)S(1)}, f32[3,4,128]{2,1,0:T(4,128)S(1)}, u32[]{:S(2)}, u32[]{:S(2)}) collective-permute-start(f32[3,4,128]{2,1,0:T(4,128)S(1)} %get-tuple-element.38), channel_id=1, source_target_pairs={{0,8},{8,16},{16,24},{24,0},{1,9},{9,17},{17,25},{25,1},{2,10},{10... | collective-permute-start | bytes 18440 | tf_op jit(solution)/shard_map/ppermute | solution.py:28
  75.5 2.2 %copy-start.1 = (bf16[4,128,1024]{2,1,0:T(8,128)(2,1)}, bf16[4,128,1024]{2,1,0:T(8,128)(2,1)S(1)}, u32[]{:S(2)}) copy-start(bf16[4,128,1024]{2,1,0:T(8,128)(2,1)S(1)} %multiply_convert_fusion.1) | copy-start | bytes 3145732
  84.9 11.3 %collective-permute-start.6 = (bf16[128,1024]{1,0:T(8,128)(2,1)}, bf16[128,1024]{1,0:T(8,128)(2,1)S(1)}, u32[]{:S(2)}, u32[]{:S(2)}) collective-permute-start(bf16[128,1024]{1,0:T(8,128)(2,1)} %get-tuple-element.36), channel_id=1, source_target_pairs={{0,8},{8,16},{16,24},{24,0},{1,9},{9,17},{17,25},{25,1},{2,10},{10... | collective-permute-start | bytes 786440 | tf_op jit(solution)/shard_map/ppermute | solution.py:39
  84.9 20.2 %collective-permute-start.7 = (bf16[128,1024]{1,0:T(8,128)(2,1)}, bf16[128,1024]{1,0:T(8,128)(2,1)S(1)}, u32[]{:S(2)}, u32[]{:S(2)}) collective-permute-start(bf16[128,1024]{1,0:T(8,128)(2,1)} %get-tuple-element.35), channel_id=1, source_target_pairs={{0,16},{8,24},{16,0},{24,8},{1,17},{9,25},{17,1},{25,9},{2,18},{10... | collective-permute-start | bytes 786440 | tf_op jit(solution)/shard_map/ppermute | solution.py:39
  85.4 19.6 %collective-permute-start.8 = (bf16[128,1024]{1,0:T(8,128)(2,1)}, bf16[128,1024]{1,0:T(8,128)(2,1)S(1)}, u32[]{:S(2)}, u32[]{:S(2)}) collective-permute-start(bf16[128,1024]{1,0:T(8,128)(2,1)} %get-tuple-element.34), channel_id=1, source_target_pairs={{0,24},{8,0},{16,8},{24,16},{1,25},{9,1},{17,9},{25,17},{2,26},{10... | collective-permute-start | bytes 786440 | tf_op jit(solution)/shard_map/ppermute | solution.py:39
  106.2 4.5 %copy-start.4 = (f32[128,1024]{1,0:T(8,128)S(1)}, f32[128,1024]{1,0:T(8,128)}, u32[]{:S(2)}) copy-start(f32[128,1024]{1,0:T(8,128)} %copy-done.3) | copy-start | bytes 1572868
  112.7 50.5 %all-to-all-start.2 = ((bf16[8,128,1024]{2,1,0:T(8,128)(2,1)}), bf16[8,128,1024]{2,1,0:T(8,128)(2,1)}, u32[]{:S(2)}, u32[]{:S(2)}) async-start(bf16[8,128,1024]{2,1,0:T(8,128)(2,1)} %broadcast_in_dim.134), calls=%async_computation.2 | async-start | bytes 4194304 | tf_op jit(solution)/shard_map/all_to_all | solution.py:132
  117.1 79.1 %reduce-scatter.2.cloned.1.call-start = ((), (), s32[]{:S(2)}) async-start(), calls=%async_computation.6 | async-start | bytes 1310720 | tf_op jit(solution)/shard_map/reduce_scatter | solution.py:145
  157.7 4.0 %copy-start = (f32[1024,1024]{1,0:T(8,128)S(1)}, f32[1024,1024]{1,0:T(8,128)}, u32[]{:S(2)}) copy-start(f32[1024,1024]{1,0:T(8,128)} %all-gather.2.cloned.1.call-done) | copy-start | bytes 12582916
  157.7 4.7 %copy-start.2 = (bf16[1024,1024]{1,0:T(8,128)(2,1)S(1)}, bf16[1024,1024]{1,0:T(8,128)(2,1)}, u32[]{:S(2)}) copy-start(bf16[1024,1024]{1,0:T(8,128)(2,1)} %all-reduce.2.cloned.1.call-done) | copy-start | bytes 6291460
  (1 other events, 0.7 us)
Sparse Core Ops, SparseCore 0:
  13.2 39.2 all-gather.1
  88.8 68.7 all-reduce.1
  169.5 26.6 reduce-scatter.1
where the time goes:
time: 205 us
  waiting for transfers between devices  86.3 us (42%)
  matrix products  43.5 us (21%)
  starting transfers between devices  27.8 us (14%)
  other arithmetic  17.9 us (9%)
  local copies, waits for them, and re-layouts  15 us (7%)
  between operations  14 us (7%)
    psum x1, waiting for transfers between devices, body(): code_delta = lax.psum(code_sum, 'member').astype(jnp.float32)  37.8 us
    ppermute x3, waiting for transfers between devices, exchange(): lax.ppermute(sent, axis, [(i, (i + s) % size) for i in range(size)])  16.4 us
    all_gather x1, waiting for transfers between devices, body(): lax.all_gather(jnp.dot(code_feat, projection, preferred_element_type=jnp....  15 us
    reduce_scatter x1, waiting for transfers between devices, body(): lax.psum_scatter(sent_proj, 'group', scatter_dimension=0, tiled=True)  12.3 us
    ppermute x6, starting transfers between devices, shift_all(): lax.ppermute(x, axis, [(i, (i + s) % size) for i in range(size)])  11.5 us
    dot_general x1, matrix products, body(): jnp.einsum('qe,de->qd', dz_query, projection, preferred_element_type=jnp....  7.24 us
    dot_general x1, matrix products, body(): jnp.einsum('qe,de->qd', dz_code, projection, preferred_element_type=jnp.f...  7.24 us
    dot_general x1, matrix products, body(): jnp.dot(code_feat, projection, preferred_element_type=jnp.float32)  5.85 us
  transfers between devices with their start and end apart: 15, of which 8 were waited for; matrix products, arithmetic and copies ran while one was open for 30% of the time, Pallas kernels for 0%

commit v1 on v0

--- a/solution.py
+++ b/solution.py
@@ -6,6 +6,28 @@
 CB = 64
 inverse_temp = 120.0
 epsilon = 1e-06
+
+
+def joined_along(blocks, dim):
+    blocks = jnp.moveaxis(blocks, 0, dim)
+    dims = blocks.shape
+    return blocks.reshape(*dims[:dim], dims[dim] * dims[dim + 1], *dims[dim + 2 :])
+
+
+def gather_around(x, axis, dim):
+    size = lax.axis_size(axis)
+    pairs = [(i, (i + 1) % size) for i in range(size)]
+    back = [(b, a) for a, b in pairs]
+    lower, upper = ([], [])
+    for step in range(size - 1):
+        if step % 2 == 0:
+            lower.append(lax.ppermute(lower[-1] if lower else x, axis, pairs))
+        else:
+            upper.append(lax.ppermute(upper[-1] if upper else x, axis, back))
+    blocks = jnp.stack([*lower[::-1], x, *upper])
+    shift = lax.axis_index(axis) - len(lower)
+    blocks = blocks[(jnp.arange(size) - shift) % size]
+    return joined_along(blocks, dim)
 
 
 def embed(features, projection):
@@ -59,11 +81,8 @@
     feats = jnp.transpose(feats, (3, 0, 1, 2, 4))
     feat_cols = lax.all_to_all(feats, "member", split_axis=0, concat_axis=0, tiled=True)
     q_unit, q_inv, q_emb = embed(query_feat, projection)
-    code_values = lax.all_gather(
-        jnp.dot(code_feat, projection, preferred_element_type=jnp.float32),
-        "member",
-        axis=0,
-        tiled=True,
+    code_values = gather_around(
+        jnp.dot(code_feat, projection, preferred_element_type=jnp.float32), "member", 0
     )
     c_inv = lax.rsqrt(jnp.sum(code_values * code_values, axis=1) + epsilon)
     c_unit = code_values * c_inv[:, None]

time: 205 us -> 243 us (1.19)
  local copies, waits for them, and re-layouts: 15 us -> 32.4 us
  starting transfers between devices: 27.8 us -> 37.3 us
  other arithmetic: 17.9 us -> 23 us
  waiting for transfers between devices: 86.3 us -> 90.8 us
    ppermute x0 -> x7, waiting for transfers between devices: none -> 20.4 us  [the longest x3 10.4 us: gather_around(): upper.append(lax.ppermute(upper[-1] if upper else x, axis, back))]
    all_gather x1 -> x0, waiting for transfers between devices: 15 us -> none  [body(): lax.all_gather(jnp.dot(code_feat, projection, preferred_element_type=jnp....]
    unnamed x22 -> x31, local copies, waits for them, and re-layouts: 3.84 us -> 16.9 us
    ppermute x0 -> x7, starting transfers between devices: none -> 8.82 us  [the longest x3 8.26 us: gather_around(): upper.append(lax.ppermute(upper[-1] if upper else x, axis, back))]
    gather x0 -> x1, local copies, waits for them, and re-layouts: none -> 4.95 us  [gather_around(): blocks = blocks[(jnp.arange(size) - shift) % size]]
    dot_general x4, matrix products: 4.6 us -> 8.56 us  [body(): term = jnp.dot(grad[g].T, q_all[g], preferred_element_type=jnp.float32)]
    dot_general x1, matrix products: 4.98 us -> 1.4 us  [embed(): values = jnp.dot(features, projection, preferred_element_type=jnp.float32)]
    ppermute x6, waiting for transfers between devices: 4.84 us -> 2.17 us  [shift_all(): lax.ppermute(x, axis, [(i, (i + s) % size) for i in range(size)])]
  transfers between devices with their start and end apart: 15 -> 21, of which waited for: 8 -> 9; matrix products, arithmetic and copies ran while one was open for 30% -> 34% of each run, Pallas kernels for 0% -> 0%
where the time goes in v1:
time: 243 us; the launch traced here: 242 us
  waiting for transfers between devices  90.8 us (37%)
  matrix products  44.3 us (18%)
  starting transfers between devices  37.3 us (15%)
  local copies, waits for them, and re-layouts  32.4 us (13%)
  other arithmetic  23 us (9%)
  between operations  14.4 us (6%)
    psum x1, waiting for transfers between devices, body(): code_delta = lax.psum(code_sum, 'member').astype(jnp.float32)  36.9 us
    unnamed x31, local copies, waits for them, and re-layouts  16.9 us
    ppermute x3, waiting for transfers between devices, exchange(): lax.ppermute(sent, axis, [(i, (i + s) % size) for i in range(size)])  16.8 us
    reduce_scatter x1, waiting for transfers between devices, body(): lax.psum_scatter(sent_proj, 'group', scatter_dimension=0, tiled=True)  14.5 us
    ppermute x6, starting transfers between devices, shift_all(): lax.ppermute(x, axis, [(i, (i + s) % size) for i in range(size)])  12.1 us
    ppermute x3, waiting for transfers between devices, gather_around(): upper.append(lax.ppermute(upper[-1] if upper else x, axis, back))  10.4 us
    ppermute x4, waiting for transfers between devices, gather_around(): lower.append(lax.ppermute(lower[-1] if lower else x, axis, pairs))  10 us
    dot_general x4, matrix products, body(): term = jnp.dot(grad[g].T, q_all[g], preferred_element_type=jnp.float32)  8.56 us
  transfers between devices with their start and end apart: 21, of which 9 were waited for; matrix products, arithmetic and copies ran while one was open for 34% of the time, Pallas kernels for 0%

profile of v1, /device:TPU:0, one launch (start us, length us, event | category | flops | bytes accessed | tf_op | source)
XLA Modules:
  0.0 242.1 jit_solution(17948256348385657618)
XLA Ops:
  7.2 5.9 %fusion.31 = f32[128,1024]{1,0:T(8,128)} fusion(bf16[128,4096]{1,0:T(8,128)(2,1)} %param.10, bf16[4096,1024]{1,0:T(8,128)(2,1)} %param.11), kind=kOutput, calls=%fused_computation.110 | convolution fusion | flops 1073741824 | bytes 9961472 | tf_op jit(solution)/shard_map/dot_general | solution.py:85
  13.6 2.9 %collective-permute-start.7 = (f32[128,1024]{1,0:T(8,128)}, f32[128,1024]{1,0:T(8,128)}, u32[]{:S(2)}, u32[]{:S(2)}) collective-permute-start(f32[128,1024]{1,0:T(8,128)} %fusion.31), channel_id=1, source_target_pairs={{1,0},{2,1},{3,2},{4,3},{5,4},{6,5},{7,6},{0,7},{9,8},{10,9},{11,1... | collective-permute-start | bytes 1572872 | tf_op jit(solution)/shard_map/ppermute | solution.py:26
  25.4 4.3 %all-to-all-start = ((bf16[4,128,1024]{2,1,0:T(8,128)(2,1)}), bf16[4,128,1024]{2,1,0:T(8,128)(2,1)}, u32[]{:S(2)}, u32[]{:S(2)}) async-start(bf16[4,128,1024]{2,1,0:T(8,128)(2,1)} %broadcast_in_dim.127), calls=%async_computation | async-start | bytes 2097152 | tf_op jit(solution)/shard_map/all_to_all | solution.py:90
  29.8 9.5 %collective-permute-done.4 = f32[128,1024]{1,0:T(8,128)} collective-permute-done((f32[128,1024]{1,0:T(8,128)S(1)}, f32[128,1024]{1,0:T(8,128)}, u32[]{:S(2)}, u32[]{:S(2)}) %collective-permute-start.4) | collective-permute-done | bytes 524320 | tf_op jit(solution)/shard_map/ppermute | solution.py:24
  46.0 2.7 %collective-permute-start.8 = (f32[128,1024]{1,0:T(8,128)}, f32[128,1024]{1,0:T(8,128)S(1)}, u32[]{:S(2)}, u32[]{:S(2)}) collective-permute-start(f32[128,1024]{1,0:T(8,128)} %collective-permute-done.7), channel_id=1, source_target_pairs={{1,0},{2,1},{3,2},{4,3},{5,4},{6,5},{7,6},{0,7},{9,8},{10,9},{11,1... | collective-permute-start | bytes 1572872 | tf_op jit(solution)/shard_map/ppermute | solution.py:26
  49.6 10.4 %collective-permute-done.8 = f32[128,1024]{1,0:T(8,128)S(1)} collective-permute-done((f32[128,1024]{1,0:T(8,128)}, f32[128,1024]{1,0:T(8,128)S(1)}, u32[]{:S(2)}, u32[]{:S(2)}) %collective-permute-start.8) | collective-permute-done | bytes 524320 | tf_op jit(solution)/shard_map/ppermute | solution.py:26
  60.0 2.7 %collective-permute-start.9 = (f32[128,1024]{1,0:T(8,128)S(1)}, f32[128,1024]{1,0:T(8,128)S(1)}, u32[]{:S(2)}, u32[]{:S(2)}) collective-permute-start(f32[128,1024]{1,0:T(8,128)S(1)} %collective-permute-done.8), channel_id=1, source_target_pairs={{1,0},{2,1},{3,2},{4,3},{5,4},{6,5},{7,6},{0,7},{9,8},{10,9},{11,1... | collective-permute-start | bytes 1572872 | tf_op jit(solution)/shard_map/ppermute | solution.py:26
  74.8 4.9 %gather_fusion.1 = f32[8,128,1024]{2,1,0:T(8,128)} fusion(f32[8,128,1024]{2,1,0:T(8,128)} %bitcast_dynamic-update-slice_fusion, s32[1024]{0:T(1024)S(1)} %pad_clamp_fusion), kind=kCustom, calls=%fused_computation.1 | custom fusion | bytes 8388640 | tf_op jit(solution)/shard_map/gather | solution.py:29
  84.9 3.6 %all-to-all-start.1 = ((bf16[8,2,128,4,128]{2,4,3,1,0:T(8,128)(2,1)}), bf16[8,2,128,4,128]{2,4,3,1,0:T(8,128)(2,1)S(1)}, u32[]{:S(2)}, u32[]{:S(2)}) async-start(bf16[8,2,128,4,128]{2,4,3,1,0:T(8,128)(2,1)} %copy.25), calls=%async_computation.1 | async-start | bytes 4194304 | tf_op jit(solution)/shard_map/all_to_all | solution.py:82
  88.5 3.3 %fusion.29 = (f32[4,128]{1,0:T(4,128)S(1)}, f32[4,128,1024]{2,1,0:T(8,128)S(1)}) fusion(bf16[4,128,1024]{2,1,0:T(8,128)(2,1)} %all-to-all-done, bf16[1024,1024]{1,0:T(8,128)(2,1)} %fusion.3, pred[4,1024]{1,0:T(4,128)(4,1)S(1)} %broadcast_in_dim.125), kind=kOutput, calls=%fused_computation.108 | convolution fusion | flops 1075314176 | bytes 5249024 | tf_op jit(solution)/shard_map/gqe,ke->gqk/dot_general | solution.py:105
  109.8 3.3 %add_convert_fusion = bf16[1024,1024]{1,0:T(8,128)(2,1)} fusion(f32[1024,1024]{1,0:T(8,128)S(1)} %fusion.13, f32[1024,1024]{1,0:T(8,128)S(1)} %fusion.14, f32[1024,1024]{1,0:T(8,128)S(1)} %fusion.15, pred[]{:T(512)S(6)} %eq.77, pred[]{:T(512)S(6)} %eq.76, pred[]{:T(512)S(6)} %eq.75, pred[]{:T(512)S(6)} %eq.74, bf16[4,128,1024]{2,1,0:T(8,128)(2,1)} %all-to-all-done, ...), kind=kOutput, calls=%fused_computation.12 | convolution fusion | flops 285212672 | bytes 15204356 | tf_op jit(solution)/shard_map/dot_general | solution.py:130
  113.2 4.5 %fusion.30 = (bf16[4,128,1024]{2,1,0:T(8,128)(2,1)S(1)}, f32[4,128,1024]{2,1,0:T(8,128)}) fusion(bf16[4,128,1024]{2,1,0:T(8,128)(2,1)} %copy-done.7, bf16[1024,1024]{1,0:T(8,128)(2,1)} %fusion.3), kind=kOutput, calls=%fused_computation.109 | convolution fusion | flops 1074266112 | bytes 6291456 | tf_op jit(solution)/shard_map/gqk,ke->gqe/dot_general | solution.py:136
  118.6 3.7 %collective-permute-start.14 = (bf16[128,1024]{1,0:T(8,128)(2,1)S(1)}, bf16[128,1024]{1,0:T(8,128)(2,1)}, u32[]{:S(2)}, u32[]{:S(2)}) collective-permute-start(bf16[128,1024]{1,0:T(8,128)(2,1)S(1)} %get-tuple-element.35), channel_id=1, source_target_pairs={{0,16},{8,24},{16,0},{24,8},{1,17},{9,25},{17,1},{25,9},{2,18},{10... | collective-permute-start | bytes 786440 | tf_op jit(solution)/shard_map/ppermute | solution.py:61
  122.3 7.5 %collective-permute-done.13 = bf16[128,1024]{1,0:T(8,128)(2,1)} collective-permute-done((bf16[128,1024]{1,0:T(8,128)(2,1)}, bf16[128,1024]{1,0:T(8,128)(2,1)}, u32[]{:S(2)}, u32[]{:S(2)}) %collective-permute-start.13) | collective-permute-done | bytes 262176 | tf_op jit(solution)/shard_map/ppermute | solution.py:61
  129.9 9.2 %collective-permute-done.14 = bf16[128,1024]{1,0:T(8,128)(2,1)} collective-permute-done((bf16[128,1024]{1,0:T(8,128)(2,1)S(1)}, bf16[128,1024]{1,0:T(8,128)(2,1)}, u32[]{:S(2)}, u32[]{:S(2)}) %collective-permute-start.14) | collective-permute-done | bytes 262176 | tf_op jit(solution)/shard_map/ppermute | solution.py:61
  141.3 2.8 %gather_fusion.3 = bf16[4,128,1024]{2,1,0:T(8,128)(2,1)} fusion(bf16[4,128,1024]{2,1,0:T(8,128)(2,1)} %pad_maximum_fusion, s32[1024]{0:T(1024)S(1)} %pad_clamp_fusion.1), kind=kCustom, calls=%fused_computation.3 | custom fusion | bytes 2097168 | tf_op jit(solution)/shard_map/jit(_take)/gather | solution.py:63
  149.9 4.4 %all-to-all-start.2 = ((bf16[8,128,1024]{2,1,0:T(8,128)(2,1)}), bf16[8,128,1024]{2,1,0:T(8,128)(2,1)}, u32[]{:S(2)}, u32[]{:S(2)}) async-start(bf16[8,128,1024]{2,1,0:T(8,128)(2,1)} %broadcast_in_dim.135), calls=%async_computation.2 | async-start | bytes 4194304 | tf_op jit(solution)/shard_map/all_to_all | solution.py:151
  155.7 36.9 %all-reduce.2.cloned.1.call-done = bf16[1024,1024]{1,0:T(8,128)(2,1)} async-done(((bf16[1024,1024]{1,0:T(8,128)(2,1)}), bf16[1024,1024]{1,0:T(8,128)(2,1)}) %all-reduce.2.cloned.1.call-update) | async-done | bytes 2097168 | tf_op jit(solution)/shard_map/psum | solution.py:135
  192.6 3.7 %fusion = f32[1024]{0:T(1024)S(1)} fusion(bf16[1024,1024]{1,0:T(8,128)(2,1)} %all-reduce.2.cloned.1.call-done, f32[8,128,1024]{2,1,0:T(8,128)} %gather_fusion.1, f32[1024]{0:T(1024)S(1)} %rsqrt_bitcast_fusion), kind=kLoop, calls=%fused_computation.8 | loop fusion | flops 4193280 | bytes 6299648 | tf_op jit(solution)/shard_map/reduce_sum | solution.py:41
  198.1 3.2 %fusion.4 = f32[4,128,1024,1]{2,1,3,0:T(8,128)S(1)} fusion(bf16[8,128,1024]{2,1,0:T(8,128)(2,1)} %all-to-all-done.2, bf16[8,1,128,4,128]{2,4,3,1,0:T(8,128)(2,1)} %get-tuple-element.32), kind=kOutput, calls=%fused_computation.17 | convolution fusion | flops 1073741824 | bytes 5242880 | tf_op jit(solution)/shard_map/mqgr,mqe->gre/dot_general | solution.py:159
  201.3 2.9 %select_convert_fusion = (bf16[4,128,1024]{2,1,0:T(8,128)(2,1)}, f32[4,128,1024]{2,1,0:T(8,128)}) fusion(pred[4]{0:T(512)(128)(4,1)S(1)} %iota_compare_fusion.1, bf16[8,128,1024,1]{2,1,0,3:T(8,128)(2,1)S(1)} %bitcast.147, bf16[8,1,128,4,128]{2,4,3,1,0:T(8,128)(2,1)S(1)} %get-tuple-element.31, f32[4,128,1024,1]{2,1,3,0:T(8,128)S(1)} %fusion.4), kind=kOutput, calls=%fused_computation.23 | convolution fusion | flops 1074790400 | bytes 8388612 | tf_op jit(solution)/shard_map/mqgr,mqe->gre/dot_general | solution.py:161
  204.3 7.2 %convolution_convert_fusion.1 = bf16[128,4096]{1,0:T(8,128)(2,1)} fusion(bf16[128,1024]{1,0:T(8,128)(2,1)S(1)} %multiply_convert_fusion.1, bf16[4096,1024]{1,0:T(8,128)(2,1)} %param.11), kind=kOutput, calls=%fused_computation.7 | convolution fusion | flops 1074266112 | bytes 9699328 | tf_op jit(solution)/shard_map/qe,de->qd/dot_general | solution.py:145
  211.5 7.3 %convolution_convert_fusion = bf16[128,4096]{1,0:T(8,128)(2,1)} fusion(bf16[4096,1024]{1,0:T(8,128)(2,1)} %param.11, bf16[1024,1024]{1,0:T(8,128)(2,1)S(1)} %fusion.2, s32[]{:T(128)S(6)} %select_n.178), kind=kOutput, calls=%fused_computation.6 | convolution fusion | flops 1074266112 | bytes 9699332 | tf_op jit(solution)/shard_map/qe,de->qd/dot_general | solution.py:148
  218.8 14.5 %reduce-scatter.2.cloned.1.call-done = bf16[1,128,1024]{2,1,0:T(8,128)(2,1)} async-done(((bf16[4,128,1024]{2,1,0:T(8,128)(2,1)}), bf16[1,128,1024]{2,1,0:T(8,128)(2,1)}) %reduce-scatter.2.cloned.1.call-update) | async-done | bytes 262160 | tf_op jit(solution)/shard_map/reduce_scatter | solution.py:164
  (113 shorter events, 66.3 us)
Async XLA Ops:
  7.2 15.6 %copy-start = (bf16[4096,1024]{1,0:T(8,128)(2,1)S(1)}, bf16[4096,1024]{1,0:T(8,128)(2,1)}, u32[]{:S(2)}) copy-start(bf16[4096,1024]{1,0:T(8,128)(2,1)} %param.11) | copy-start | bytes 25165828
  7.2 15.6 %copy-start.5 = (bf16[128,4096]{1,0:T(8,128)(2,1)S(1)}, bf16[128,4096]{1,0:T(8,128)(2,1)}, u32[]{:S(2)}) copy-start(bf16[128,4096]{1,0:T(8,128)(2,1)} %param.9) | copy-start | bytes 3145732
  13.1 16.6 %collective-permute-start.3 = (f32[128,1024]{1,0:T(8,128)}, f32[128,1024]{1,0:T(8,128)S(1)}, u32[]{:S(2)}, u32[]{:S(2)}) collective-permute-start(f32[128,1024]{1,0:T(8,128)} %fusion.31), channel_id=1, source_target_pairs={{0,1},{1,2},{2,3},{3,4},{4,5},{5,6},{6,7},{7,0},{8,9},{9,10},{10,1... | collective-permute-start | bytes 1572872 | tf_op jit(solution)/shard_map/ppermute | solution.py:24
  13.6 32.4 %collective-permute-start.7 = (f32[128,1024]{1,0:T(8,128)}, f32[128,1024]{1,0:T(8,128)}, u32[]{:S(2)}, u32[]{:S(2)}) collective-permute-start(f32[128,1024]{1,0:T(8,128)} %fusion.31), channel_id=1, source_target_pairs={{1,0},{2,1},{3,2},{4,3},{5,4},{6,5},{7,6},{0,7},{9,8},{10,9},{11,1... | collective-permute-start | bytes 1572872 | tf_op jit(solution)/shard_map/ppermute | solution.py:26
  16.5 28.9 %collective-permute-start = (s32[16]{0:T(128)S(1)}, s32[16]{0:T(128)S(1)}, u32[]{:S(2)}, u32[]{:S(2)}) collective-permute-start(s32[16]{0:T(128)S(1)} %bitcast.156), channel_id=1, source_target_pairs={{0,8},{8,16},{16,24},{24,0},{1,9},{9,17},{17,25},{25,1},{2,10},{10... | collective-permute-start | bytes 200 | tf_op jit(solution)/shard_map/ppermute | solution.py:50
  18.8 26.6 %collective-permute-start.1 = (s32[16]{0:T(128)S(1)}, s32[16]{0:T(128)S(1)}, u32[]{:S(2)}, u32[]{:S(2)}) collective-permute-start(s32[16]{0:T(128)S(1)} %bitcast.157), channel_id=1, source_target_pairs={{0,16},{8,24},{16,0},{24,8},{1,17},{9,25},{17,1},{25,9},{2,18},{10... | collective-permute-start | bytes 200 | tf_op jit(solution)/shard_map/ppermute | solution.py:50
  21.4 24.0 %collective-permute-start.2 = (s32[16]{0:T(128)S(1)}, s32[16]{0:T(128)S(1)}, u32[]{:S(2)}, u32[]{:S(2)}) collective-permute-start(s32[16]{0:T(128)S(1)} %bitcast.158), channel_id=1, source_target_pairs={{0,24},{8,0},{16,8},{24,16},{1,25},{9,1},{17,9},{25,17},{2,26},{10... | collective-permute-start | bytes 200 | tf_op jit(solution)/shard_map/ppermute | solution.py:50
  24.1 16.5 %copy-start.6 = (bf16[128,4096]{1,0:T(8,128)(2,1)S(1)}, bf16[128,4096]{1,0:T(8,128)(2,1)}, u32[]{:S(2)}) copy-start(bf16[128,4096]{1,0:T(8,128)(2,1)} %param.10) | copy-start | bytes 3145732
  25.4 59.5 %all-to-all-start = ((bf16[4,128,1024]{2,1,0:T(8,128)(2,1)}), bf16[4,128,1024]{2,1,0:T(8,128)(2,1)}, u32[]{:S(2)}, u32[]{:S(2)}) async-start(bf16[4,128,1024]{2,1,0:T(8,128)(2,1)} %broadcast_in_dim.127), calls=%async_computation | async-start | bytes 2097152 | tf_op jit(solution)/shard_map/all_to_all | solution.py:90
  29.7 9.7 %collective-permute-start.4 = (f32[128,1024]{1,0:T(8,128)S(1)}, f32[128,1024]{1,0:T(8,128)}, u32[]{:S(2)}, u32[]{:S(2)}) collective-permute-start(f32[128,1024]{1,0:T(8,128)S(1)} %collective-permute-done.3), channel_id=1, source_target_pairs={{0,1},{1,2},{2,3},{3,4},{4,5},{5,6},{6,7},{7,0},{8,9},{9,10},{10,1... | collective-permute-start | bytes 1572872 | tf_op jit(solution)/shard_map/ppermute | solution.py:24
  39.3 9.8 %collective-permute-start.5 = (f32[128,1024]{1,0:T(8,128)}, f32[128,1024]{1,0:T(8,128)}, u32[]{:S(2)}, u32[]{:S(2)}) collective-permute-start(f32[128,1024]{1,0:T(8,128)} %collective-permute-done.4), channel_id=1, source_target_pairs={{0,1},{1,2},{2,3},{3,4},{4,5},{5,6},{6,7},{7,0},{8,9},{9,10},{10,1... | collective-permute-start | bytes 1572872 | tf_op jit(solution)/shard_map/ppermute | solution.py:24
  46.0 14.0 %collective-permute-start.8 = (f32[128,1024]{1,0:T(8,128)}, f32[128,1024]{1,0:T(8,128)S(1)}, u32[]{:S(2)}, u32[]{:S(2)}) collective-permute-start(f32[128,1024]{1,0:T(8,128)} %collective-permute-done.7), channel_id=1, source_target_pairs={{1,0},{2,1},{3,2},{4,3},{5,4},{6,5},{7,6},{0,7},{9,8},{10,9},{11,1... | collective-permute-start | bytes 1572872 | tf_op jit(solution)/shard_map/ppermute | solution.py:26
  49.2 13.6 %collective-permute-start.6 = (f32[128,1024]{1,0:T(8,128)}, f32[128,1024]{1,0:T(8,128)S(1)}, u32[]{:S(2)}, u32[]{:S(2)}) collective-permute-start(f32[128,1024]{1,0:T(8,128)} %collective-permute-done.5), channel_id=1, source_target_pairs={{0,1},{1,2},{2,3},{3,4},{4,5},{5,6},{6,7},{7,0},{8,9},{9,10},{10,1... | collective-permute-start | bytes 1572872 | tf_op jit(solution)/shard_map/ppermute | solution.py:24
  60.0 13.9 %collective-permute-start.9 = (f32[128,1024]{1,0:T(8,128)S(1)}, f32[128,1024]{1,0:T(8,128)S(1)}, u32[]{:S(2)}, u32[]{:S(2)}) collective-permute-start(f32[128,1024]{1,0:T(8,128)S(1)} %collective-permute-done.8), channel_id=1, source_target_pairs={{1,0},{2,1},{3,2},{4,3},{5,4},{6,5},{7,6},{0,7},{9,8},{10,9},{11,1... | collective-permute-start | bytes 1572872 | tf_op jit(solution)/shard_map/ppermute | solution.py:26
  84.9 63.4 %all-to-all-start.1 = ((bf16[8,2,128,4,128]{2,4,3,1,0:T(8,128)(2,1)}), bf16[8,2,128,4,128]{2,4,3,1,0:T(8,128)(2,1)S(1)}, u32[]{:S(2)}, u32[]{:S(2)}) async-start(bf16[8,2,128,4,128]{2,4,3,1,0:T(8,128)(2,1)} %copy.25), calls=%async_computation.1 | async-start | bytes 4194304 | tf_op jit(solution)/shard_map/all_to_all | solution.py:82
  88.5 104.1 %all-reduce.2.cloned.1.call-start = ((), (), s32[]{:S(2)}) async-start(), calls=%async_computation.4 | async-start | bytes 4194304 | tf_op jit(solution)/shard_map/psum | solution.py:135
  93.7 5.9 %collective-permute-start.10 = (f32[3,4,128]{2,1,0:T(4,128)S(1)}, f32[3,4,128]{2,1,0:T(4,128)S(1)}, u32[]{:S(2)}, u32[]{:S(2)}) collective-permute-start(f32[3,4,128]{2,1,0:T(4,128)S(1)} %get-tuple-element.38), channel_id=1, source_target_pairs={{0,8},{8,16},{16,24},{24,0},{1,9},{9,17},{17,25},{25,1},{2,10},{10... | collective-permute-start | bytes 18440 | tf_op jit(solution)/shard_map/ppermute | solution.py:50
  95.7 4.5 %collective-permute-start.11 = (f32[3,4,128]{2,1,0:T(4,128)S(1)}, f32[3,4,128]{2,1,0:T(4,128)S(1)}, u32[]{:S(2)}, u32[]{:S(2)}) collective-permute-start(f32[3,4,128]{2,1,0:T(4,128)S(1)} %get-tuple-element.38), channel_id=1, source_target_pairs={{0,16},{8,24},{16,0},{24,8},{1,17},{9,25},{17,1},{25,9},{2,18},{10... | collective-permute-start | bytes 18440 | tf_op jit(solution)/shard_map/ppermute | solution.py:50
  98.1 3.6 %collective-permute-start.12 = (f32[3,4,128]{2,1,0:T(4,128)S(1)}, f32[3,4,128]{2,1,0:T(4,128)S(1)}, u32[]{:S(2)}, u32[]{:S(2)}) collective-permute-start(f32[3,4,128]{2,1,0:T(4,128)S(1)} %get-tuple-element.38), channel_id=1, source_target_pairs={{0,24},{8,0},{16,8},{24,16},{1,25},{9,1},{17,9},{25,17},{2,26},{10... | collective-permute-start | bytes 18440 | tf_op jit(solution)/shard_map/ppermute | solution.py:50
  118.5 11.4 %collective-permute-start.13 = (bf16[128,1024]{1,0:T(8,128)(2,1)}, bf16[128,1024]{1,0:T(8,128)(2,1)}, u32[]{:S(2)}, u32[]{:S(2)}) collective-permute-start(bf16[128,1024]{1,0:T(8,128)(2,1)} %get-tuple-element.36), channel_id=1, source_target_pairs={{0,8},{8,16},{16,24},{24,0},{1,9},{9,17},{17,25},{25,1},{2,10},{10... | collective-permute-start | bytes 786440 | tf_op jit(solution)/shard_map/ppermute | solution.py:61
  118.6 20.5 %collective-permute-start.14 = (bf16[128,1024]{1,0:T(8,128)(2,1)S(1)}, bf16[128,1024]{1,0:T(8,128)(2,1)}, u32[]{:S(2)}, u32[]{:S(2)}) collective-permute-start(bf16[128,1024]{1,0:T(8,128)(2,1)S(1)} %get-tuple-element.35), channel_id=1, source_target_pairs={{0,16},{8,24},{16,0},{24,8},{1,17},{9,25},{17,1},{25,9},{2,18},{10... | collective-permute-start | bytes 786440 | tf_op jit(solution)/shard_map/ppermute | solution.py:61
  122.3 16.8 %collective-permute-start.15 = (bf16[128,1024]{1,0:T(8,128)(2,1)S(1)}, bf16[128,1024]{1,0:T(8,128)(2,1)}, u32[]{:S(2)}, u32[]{:S(2)}) collective-permute-start(bf16[128,1024]{1,0:T(8,128)(2,1)S(1)} %get-tuple-element.34), channel_id=1, source_target_pairs={{0,24},{8,0},{16,8},{24,16},{1,25},{9,1},{17,9},{25,17},{2,26},{10... | collective-permute-start | bytes 786440 | tf_op jit(solution)/shard_map/ppermute | solution.py:61
  149.9 48.3 %all-to-all-start.2 = ((bf16[8,128,1024]{2,1,0:T(8,128)(2,1)}), bf16[8,128,1024]{2,1,0:T(8,128)(2,1)}, u32[]{:S(2)}, u32[]{:S(2)}) async-start(bf16[8,128,1024]{2,1,0:T(8,128)(2,1)} %broadcast_in_dim.135), calls=%async_computation.2 | async-start | bytes 4194304 | tf_op jit(solution)/shard_map/all_to_all | solution.py:151
  154.3 79.0 %reduce-scatter.2.cloned.1.call-start = ((), (), s32[]{:S(2)}) async-start(), calls=%async_computation.5 | async-start | bytes 1310720 | tf_op jit(solution)/shard_map/reduce_scatter | solution.py:164
  (8 other events, 45.5 us)
Sparse Core Ops, SparseCore 0:
  122.4 70.1 all-reduce.1
  204.4 28.8 reduce-scatter.1
